TPU v7x, 512 devices: a whole 4x8x8 slice. The times are simulated.
512 devices in a mesh: req: 64 (over z, x, core), voc: 8 (over y).
Axes of the slice: x: 4, y: 8, z: 8, core: 2. Of those that a mesh axis runs over, the one named last changes fastest.
Arguments:
- hidden: bfloat16 [65536, 1600], P(('req', 'voc')), may hold values from -60 to 60
- norm_gain: float32 [1600], replicated, may hold values from 0.25 to 1.75
- unembed: bfloat16 [16384, 1600], P(('req', 'voc')), may hold values from -2 to 2
- targets: int32 [65536], P(('req', 'voc')), may hold values from 0 to 16383
- live: int32 [65536], P(('req', 'voc')), may hold values from 0 to 1, as said below
Outputs:
- logprob: float32 [65536], P(('req', 'voc'))
- entropy: float32 [65536], P(('req', 'voc'))
Inputs may be any that keep to these rules, and one draw needn't show every extreme that they name: Within each aligned block of 1024 slots (one owner's) the live slots form a prefix of 128 to 1024 slots, and in every draw at least one block is wholly live.
All inputs are finite; a program needn't handle non-finite values.
Results may differ from a plain program's by a relative error of at most 0.0067.
Values may be sent and summed in bfloat16 or wider, within the bound.
No kernel may reach another device: no remote copies, remote signals or barrier semaphores. Data moves between devices by JAX's collectives and lax.ppermute only.
A program may use at most 64 MiB of HBM per device.

v0:
```python
import jax
import jax.numpy as jnp
from jax import lax
from jax.sharding import Mesh, PartitionSpec as P

FLAT = ("z", "x", "c", "y")


def combine_stats(first, second):
    top = jnp.maximum(first[0], second[0])
    scale_one = jnp.exp(first[0] - top)
    scale_two = jnp.exp(second[0] - top)
    total = first[1] * scale_one + second[1] * scale_two
    spread = scale_one * (first[2] + (first[0] - top) * first[1]) + scale_two * (
        second[2] + (second[0] - top) * second[1]
    )
    return (top, total, spread, first[3] + second[3])


def shift(value, axis, size, step):
    return lax.ppermute(value, axis, [(i, (i + step) % size) for i in range(size)])


def chunk_stats(normed, piece, ids, wanted):
    logits = lax.dot_general(
        normed, piece, (((1,), (1,)), ((), ())), preferred_element_type=jnp.float32
    )
    chosen = jnp.sum(jnp.where(ids[None, :] == wanted[:, None], logits, 0.0), axis=1)
    fold_top = jnp.max(logits, axis=1)
    shifted = logits - fold_top[:, None]
    weights = jnp.exp(shifted)
    return (fold_top, jnp.sum(weights, axis=1), jnp.sum(weights * shifted, axis=1), chosen)


def on_device(hidden, norm_gain, unembed, targets, live):
    ny = lax.axis_size("y")
    nc = lax.axis_size("c")
    y = lax.axis_index("y")
    c = lax.axis_index("c")
    mine = hidden.shape[0]
    width = unembed.shape[0]
    wide = hidden.astype(jnp.float32)
    normed = (
        wide * lax.rsqrt(jnp.mean(wide * wide, axis=1, keepdims=True) + 1e-06) * norm_gain
    ).astype(jnp.bfloat16)
    blocks = [None] * ny
    blocks[0] = (normed, targets)
    fwd = ny // 2
    cur = (normed, targets)
    for d in range(1, fwd + 1):
        cur = shift(cur, "y", ny, 1)
        blocks[ny - d] = cur
    cur = (normed, targets)
    for d in range(1, ny - fwd):
        cur = shift(cur, "y", ny, -1)
        blocks[d] = cur
    rows = jnp.concatenate([b[0] for b in blocks], axis=0)
    wanted = jnp.concatenate([b[1] for b in blocks], axis=0)
    half = lax.all_gather(unembed, ("z", "x"), axis=0, tiled=True)
    other = shift(half, "c", nc, 1)

    def ids_of(core):
        local = jnp.arange(half.shape[0], dtype=jnp.int32)
        return (local // width * (nc * ny) + core * ny + y) * width + local % width

    count = rows.shape[0]
    zeros = jnp.zeros((count,), jnp.float32)
    stats = (jnp.full((count,), -1e30, jnp.float32), zeros, zeros, zeros)
    step = min(512, half.shape[0])
    for table, core in ((half, c), (other, (c + 1) % nc)):
        ids = ids_of(core)
        for first in range(0, table.shape[0], step):
            stats = combine_stats(
                stats,
                chunk_stats(rows, table[first : first + step], ids[first : first + step], wanted),
            )
    packed = jnp.stack(stats).reshape(4, ny, mine)
    merged = tuple(packed[:, 0])
    for d in range(1, ny):
        got = shift(packed[:, d], "y", ny, d)
        merged = combine_stats(merged, tuple(got))
    top, total, spread, picked = merged
    mask = live.astype(jnp.float32)
    logprob = (picked - top - jnp.log(total)) * mask
    entropy = (jnp.log(total) - spread / total) * mask
    return (logprob, entropy)


def solution(mesh):
    nz, nx, nc = (8, 4, 2)
    ny = mesh.devices.shape[1]
    req = mesh.devices.shape[0]
    nz = req // (nx * nc)
    flat = Mesh(mesh.devices.reshape(nz, nx, nc, ny), FLAT)
    return jax.shard_map(
        on_device,
        mesh=flat,
        in_specs=(P(FLAT, None), P(), P(FLAT, None), P(FLAT), P(FLAT)),
        out_specs=(P(FLAT), P(FLAT)),
        check_vma=False,
    )
```

profile of v0, /device:TPU:56, one launch (start us, length us, event | category | flops | bytes accessed | tf_op | source)
XLA Modules:
  0.0 202.6 jit_solution(11467726991118370099)
XLA Ops:
  7.2 0.0 all-gather.2.cloned.1.call-start
  7.2 0.7 all-gather.2.cloned.1.call-update
  7.9 1.2 fusion.12
  9.1 2.2 %constant_dynamic-update-slice_fusion.8 = (bf16[1024,1600]{0,1:T(8,128)(2,1)}, bf16[128,1600]{0,1:T(8,128)(2,1)}) fusion(f32[1600]{0:T(1024)} %param.6, f32[128]{0:T(128)S(1)} %add_rsqrt_fusion, bf16[128,1600]{0,1:T(8,128)(2,1)} %param.5), kind=kLoop, calls=%fused_computation.37 | loop fusion | flops 819199 | bytes 1235712
  11.4 3.2 %collective-permute-start.7 = (bf16[128,1600]{0,1:T(8,128)(2,1)}, bf16[128,1600]{0,1:T(8,128)(2,1)}, u32[]{:S(2)}, u32[]{:S(2)}) collective-permute-start(bf16[128,1600]{0,1:T(8,128)(2,1)} %get-tuple-element.18), channel_id=1, source_target_pairs={{0,7},{1,0},{2,1},{3,2},{4,3},{5,4},{6,5},{7,6},{8,15},{9,8},{10,9... | collective-permute-start | bytes 1228808 | tf_op jit(solution)/shard_map/ppermute | solution.py:21
  14.6 5.7 %collective-permute-start.10 = (bf16[128,1600]{0,1:T(8,128)(2,1)}, bf16[128,1600]{0,1:T(8,128)(2,1)}, u32[]{:S(2)}, u32[]{:S(2)}) collective-permute-start(bf16[128,1600]{0,1:T(8,128)(2,1)} %get-tuple-element.18), channel_id=1, source_target_pairs={{0,1},{1,2},{2,3},{3,4},{4,5},{5,6},{6,7},{7,0},{8,9},{9,10},{10,1... | collective-permute-start | bytes 1228808 | tf_op jit(solution)/shard_map/ppermute | solution.py:21
  20.3 1.9 collective-permute-start
  22.3 5.1 %collective-permute-start.3 = (s32[128]{0:T(128)}, s32[128]{0:T(128)S(1)}, u32[]{:S(2)}, u32[]{:S(2)}) collective-permute-start(s32[128]{0:T(128)} %param.8), channel_id=1, source_target_pairs={{0,1},{1,2},{2,3},{3,4},{4,5},{5,6},{6,7},{7,0},{8,9},{9,10},{10,1... | collective-permute-start | bytes 1544 | tf_op jit(solution)/shard_map/ppermute | solution.py:21
  27.5 0.7 constant_dynamic-update-slice_fusion
  28.2 1.9 collective-permute-start.1
  30.1 5.1 %collective-permute-start.4 = (s32[128]{0:T(128)S(1)}, s32[128]{0:T(128)S(1)}, u32[]{:S(2)}, u32[]{:S(2)}) collective-permute-start(s32[128]{0:T(128)S(1)} %collective-permute-done.3), channel_id=1, source_target_pairs={{0,1},{1,2},{2,3},{3,4},{4,5},{5,6},{6,7},{7,0},{8,9},{9,10},{10,1... | collective-permute-start | bytes 1544 | tf_op jit(solution)/shard_map/ppermute | solution.py:21
  35.3 1.9 collective-permute-start.2
  37.2 5.1 %collective-permute-start.5 = (s32[128]{0:T(128)S(1)}, s32[128]{0:T(128)S(1)}, u32[]{:S(2)}, u32[]{:S(2)}) collective-permute-start(s32[128]{0:T(128)S(1)} %collective-permute-done.4), channel_id=1, source_target_pairs={{0,1},{1,2},{2,3},{3,4},{4,5},{5,6},{6,7},{7,0},{8,9},{9,10},{10,1... | collective-permute-start | bytes 1544 | tf_op jit(solution)/shard_map/ppermute | solution.py:21
  42.3 1.9 collective-permute-start.11
  44.3 4.7 %collective-permute-start.6 = (s32[128]{0:T(128)S(1)}, s32[128]{0:T(128)S(1)}, u32[]{:S(2)}, u32[]{:S(2)}) collective-permute-start(s32[128]{0:T(128)S(1)} %collective-permute-done.5), channel_id=1, source_target_pairs={{0,1},{1,2},{2,3},{3,4},{4,5},{5,6},{6,7},{7,0},{8,9},{9,10},{10,1... | collective-permute-start | bytes 1544 | tf_op jit(solution)/shard_map/ppermute | solution.py:21
  49.0 52.7 %all-gather.2.cloned.1.call-done = bf16[1024,1600]{1,0:T(8,128)(2,1)} async-done(((bf16[32,1600]{1,0:T(8,128)(2,1)}), bf16[1024,1600]{1,0:T(8,128)(2,1)}) %all-gather.2.cloned.1.call-update) | async-done | bytes 3276816 | tf_op jit(solution)/shard_map/all_gather | solution.py:59
  101.7 4.3 %copy.9 = bf16[1024,1600]{0,1:T(8,128)(2,1)S(1)} copy(bf16[1024,1600]{1,0:T(8,128)(2,1)} %all-gather.2.cloned.1.call-done) | data formatting | bytes 6553600 | tf_op jit(solution)/shard_map/all_gather | solution.py:59
  106.0 2.2 %collective-permute-start.14 = (bf16[1024,1600]{0,1:T(8,128)(2,1)S(1)}, bf16[1024,1600]{0,1:T(8,128)(2,1)S(1)}, u32[]{:S(2)}, u32[]{:S(2)}) collective-permute-start(bf16[1024,1600]{0,1:T(8,128)(2,1)S(1)} %copy.9), channel_id=1, source_target_pairs={{0,8},{8,0},{1,9},{9,1},{2,10},{10,2},{3,11},{11,3},{4,12},{12,4},... | collective-permute-start | bytes 9830408 | tf_op jit(solution)/shard_map/ppermute | solution.py:21
  108.2 3.3 %collective-permute-start.8 = (bf16[128,1600]{0,1:T(8,128)(2,1)}, bf16[128,1600]{0,1:T(8,128)(2,1)S(1)}, u32[]{:S(2)}, u32[]{:S(2)}) collective-permute-start(bf16[128,1600]{0,1:T(8,128)(2,1)} %collective-permute-done.7), channel_id=1, source_target_pairs={{0,7},{1,0},{2,1},{3,2},{4,3},{5,4},{6,5},{7,6},{8,15},{9,8},{10,9... | collective-permute-start | bytes 1228808 | tf_op jit(solution)/shard_map/ppermute | solution.py:21
  111.6 3.7 %collective-permute-start.12 = (bf16[128,1600]{0,1:T(8,128)(2,1)}, bf16[128,1600]{0,1:T(8,128)(2,1)S(1)}, u32[]{:S(2)}, u32[]{:S(2)}) collective-permute-start(bf16[128,1600]{0,1:T(8,128)(2,1)} %collective-permute-done.11), channel_id=1, source_target_pairs={{0,1},{1,2},{2,3},{3,4},{4,5},{5,6},{6,7},{7,0},{8,9},{9,10},{10,1... | collective-permute-start | bytes 1228808 | tf_op jit(solution)/shard_map/ppermute | solution.py:21
  115.3 8.0 %collective-permute-done.8 = bf16[128,1600]{0,1:T(8,128)(2,1)S(1)} collective-permute-done((bf16[128,1600]{0,1:T(8,128)(2,1)}, bf16[128,1600]{0,1:T(8,128)(2,1)S(1)}, u32[]{:S(2)}, u32[]{:S(2)}) %collective-permute-start.8) | collective-permute-done | bytes 409632 | tf_op jit(solution)/shard_map/ppermute | solution.py:21
  123.4 2.1 %collective-permute-start.9 = (bf16[128,1600]{0,1:T(8,128)(2,1)S(1)}, bf16[128,1600]{0,1:T(8,128)(2,1)S(1)}, u32[]{:S(2)}, u32[]{:S(2)}) collective-permute-start(bf16[128,1600]{0,1:T(8,128)(2,1)S(1)} %collective-permute-done.8), channel_id=1, source_target_pairs={{0,7},{1,0},{2,1},{3,2},{4,3},{5,4},{6,5},{7,6},{8,15},{9,8},{10,9... | collective-permute-start | bytes 1228808 | tf_op jit(solution)/shard_map/ppermute | solution.py:21
  125.5 1.8 constant_dynamic-update-slice_fusion.7
  127.4 4.9 %collective-permute-start.13 = (bf16[128,1600]{0,1:T(8,128)(2,1)S(1)}, bf16[128,1600]{0,1:T(8,128)(2,1)S(1)}, u32[]{:S(2)}, u32[]{:S(2)}) collective-permute-start(bf16[128,1600]{0,1:T(8,128)(2,1)S(1)} %collective-permute-done.12), channel_id=1, source_target_pairs={{0,1},{1,2},{2,3},{3,4},{4,5},{5,6},{6,7},{7,0},{8,9},{9,10},{10,1... | collective-permute-start | bytes 1228808 | tf_op jit(solution)/shard_map/ppermute | solution.py:21
  132.3 0.8 constant_dynamic-update-slice_fusion.6
  133.1 4.5 %collective-permute-done.9 = bf16[128,1600]{0,1:T(8,128)(2,1)S(1)} collective-permute-done((bf16[128,1600]{0,1:T(8,128)(2,1)S(1)}, bf16[128,1600]{0,1:T(8,128)(2,1)S(1)}, u32[]{:S(2)}, u32[]{:S(2)}) %collective-permute-start.9) | collective-permute-done | bytes 409632 | tf_op jit(solution)/shard_map/ppermute | solution.py:21
  137.6 0.8 constant_dynamic-update-slice_fusion.5
  138.4 2.2 %collective-permute-done.13 = bf16[128,1600]{0,1:T(8,128)(2,1)S(1)} collective-permute-done((bf16[128,1600]{0,1:T(8,128)(2,1)S(1)}, bf16[128,1600]{0,1:T(8,128)(2,1)S(1)}, u32[]{:S(2)}, u32[]{:S(2)}) %collective-permute-start.13) | collective-permute-done | bytes 409632 | tf_op jit(solution)/shard_map/ppermute | solution.py:21
  140.6 0.8 constant_dynamic-update-slice_fusion.4
  141.4 0.8 constant_dynamic-update-slice_fusion.3
  142.2 1.8 constant_dynamic-update-slice_fusion.2
  144.0 1.8 constant_dynamic-update-slice_fusion.1
  145.9 4.2 %fusion.87 = (f32[1024]{0:T(1024)S(1)}, f32[1024,512]{0,1:T(8,128)S(1)}) fusion(bf16[1024,1600]{0,1:T(8,128)(2,1)} %constant_dynamic-update-slice_fusion.1, bf16[1024,1600]{1,0:T(8,128)(2,1)S(1)} %copy-done), kind=kOutput, calls=%fused_computation.198 | convolution fusion | flops 1678244864 | bytes 7081984 | tf_op jit(solution)/shard_map/dot_general | solution.py:25
  150.1 2.1 %fusion.90 = (f32[1024]{0:T(1024)S(1)}, f32[1024,512]{0,1:T(8,128)S(1)}) fusion(bf16[1024,1600]{0,1:T(8,128)(2,1)S(1)} %copy-done.1, bf16[1024,1600]{1,0:T(8,128)(2,1)S(1)} %copy-done), kind=kOutput, calls=%fused_computation.201 | convolution fusion | flops 1678244864 | bytes 7081984 | tf_op jit(solution)/shard_map/dot_general | solution.py:25
  152.2 2.1 %fusion.88 = (f32[1024]{0:T(1024)S(1)}, f32[1024,512]{0,1:T(8,128)S(1)}) fusion(bf16[1024,1600]{0,1:T(8,128)(2,1)S(1)} %copy-done.1, bf16[1024,1600]{0,1:T(8,128)(2,1)S(1)} %collective-permute-done.14), kind=kOutput, calls=%fused_computation.199 | convolution fusion | flops 1678244864 | bytes 7016448 | tf_op jit(solution)/shard_map/dot_general | solution.py:25
  154.3 2.2 %fusion.89 = (f32[1024]{0:T(1024)S(1)}, f32[1024,512]{0,1:T(8,128)S(1)}) fusion(bf16[1024,1600]{0,1:T(8,128)(2,1)S(1)} %copy-done.1, bf16[1024,1600]{0,1:T(8,128)(2,1)S(1)} %collective-permute-done.14), kind=kOutput, calls=%fused_computation.200 | convolution fusion | flops 1678244864 | bytes 7016448 | tf_op jit(solution)/shard_map/dot_general | solution.py:25
  156.5 0.0 copy-start.2
  156.5 3.9 %exponential_reduce_fusion.2 = (f32[1024]{0:T(1024)S(1)}, f32[1024]{0:T(1024)S(1)}, f32[1024]{0:T(1024)S(1)}, f32[1024]{0:T(1024)S(1)}, f32[1024]{0:T(1024)S(1)}...) fusion(f32[1024,512]{0,1:T(8,128)S(1)} %get-tuple-element.43, ...), kind=kLoop, calls=%fused_computation.5 | loop fusion | flops 14667776 | bytes 8466432 | tf_op jit(solution)/shard_map/reduce_sum | solution.py:32
  160.5 5.6 %collective-permute-start.15 = (f32[4,128]{1,0:T(4,128)S(1)}, f32[4,128]{1,0:T(4,128)S(1)}, u32[]{:S(2)}, u32[]{:S(2)}) collective-permute-start(f32[4,128]{1,0:T(4,128)S(1)} %bitcast.594), channel_id=1, source_target_pairs={{0,1},{1,2},{2,3},{3,4},{4,5},{5,6},{6,7},{7,0},{8,9},{9,10},{10,1... | collective-permute-start | bytes 6152 | tf_op jit(solution)/shard_map/ppermute | solution.py:21
  166.1 5.1 %collective-permute-start.18 = (f32[4,128]{1,0:T(4,128)S(1)}, f32[4,128]{1,0:T(4,128)S(1)}, u32[]{:S(2)}, u32[]{:S(2)}) collective-permute-start(f32[4,128]{1,0:T(4,128)S(1)} %bitcast.593), channel_id=1, source_target_pairs={{0,4},{1,5},{2,6},{3,7},{4,0},{5,1},{6,2},{7,3},{8,12},{9,13},{10,... | collective-permute-start | bytes 6152 | tf_op jit(solution)/shard_map/ppermute | solution.py:21
  171.2 2.0 collective-permute-start.19
  173.2 2.9 %collective-permute-start.20 = (f32[4,128]{1,0:T(4,128)S(1)}, f32[4,128]{1,0:T(4,128)S(1)}, u32[]{:S(2)}, u32[]{:S(2)}) collective-permute-start(f32[4,128]{1,0:T(4,128)S(1)} %bitcast.591), channel_id=1, source_target_pairs={{0,6},{1,7},{2,0},{3,1},{4,2},{5,3},{6,4},{7,5},{8,14},{9,15},{10,... | collective-permute-start | bytes 6152 | tf_op jit(solution)/shard_map/ppermute | solution.py:21
  176.1 5.0 %collective-permute-start.16 = (f32[4,128]{1,0:T(4,128)S(1)}, f32[4,128]{1,0:T(4,128)S(1)}, u32[]{:S(2)}, u32[]{:S(2)}) collective-permute-start(f32[4,128]{1,0:T(4,128)S(1)} %bitcast.597), channel_id=1, source_target_pairs={{0,2},{1,3},{2,4},{3,5},{4,6},{5,7},{6,0},{7,1},{8,10},{9,11},{10,... | collective-permute-start | bytes 6152 | tf_op jit(solution)/shard_map/ppermute | solution.py:21
  181.2 6.8 %collective-permute-start.17 = (f32[4,128]{1,0:T(4,128)S(1)}, f32[4,128]{1,0:T(4,128)S(1)}, u32[]{:S(2)}, u32[]{:S(2)}) collective-permute-start(f32[4,128]{1,0:T(4,128)S(1)} %bitcast.596), channel_id=1, source_target_pairs={{0,3},{1,4},{2,5},{3,6},{4,7},{5,0},{6,1},{7,2},{8,11},{9,12},{10,... | collective-permute-start | bytes 6152 | tf_op jit(solution)/shard_map/ppermute | solution.py:21
  188.0 1.9 collective-permute-start.21
  190.0 4.7 %collective-permute-done.21 = f32[4,128]{1,0:T(4,128)S(1)} collective-permute-done((f32[4,128]{1,0:T(4,128)S(1)}, f32[4,128]{1,0:T(4,128)S(1)}, u32[]{:S(2)}, u32[]{:S(2)}) %collective-permute-start.21) | collective-permute-done | bytes 2080 | tf_op jit(solution)/shard_map/ppermute | solution.py:21
  194.7 0.5 subtract_multiply_fusion
  195.3 0.5 fusion.82
  (39 shorter events, 0.2 us)
Async XLA Ops:
  7.2 94.5 %all-gather.2.cloned.1.call-start = ((), (), s32[]{:S(2)}) async-start(), calls=%async_computation | async-start | bytes 3514368 | tf_op jit(solution)/shard_map/all_gather | solution.py:59
  11.4 96.8 %collective-permute-start.7 = (bf16[128,1600]{0,1:T(8,128)(2,1)}, bf16[128,1600]{0,1:T(8,128)(2,1)}, u32[]{:S(2)}, u32[]{:S(2)}) collective-permute-start(bf16[128,1600]{0,1:T(8,128)(2,1)} %get-tuple-element.18), channel_id=1, source_target_pairs={{0,7},{1,0},{2,1},{3,2},{4,3},{5,4},{6,5},{7,6},{8,15},{9,8},{10,9... | collective-permute-start | bytes 1228808 | tf_op jit(solution)/shard_map/ppermute | solution.py:21
  14.6 27.7 %collective-permute-start.10 = (bf16[128,1600]{0,1:T(8,128)(2,1)}, bf16[128,1600]{0,1:T(8,128)(2,1)}, u32[]{:S(2)}, u32[]{:S(2)}) collective-permute-start(bf16[128,1600]{0,1:T(8,128)(2,1)} %get-tuple-element.18), channel_id=1, source_target_pairs={{0,1},{1,2},{2,3},{3,4},{4,5},{5,6},{6,7},{7,0},{8,9},{9,10},{10,1... | collective-permute-start | bytes 1228808 | tf_op jit(solution)/shard_map/ppermute | solution.py:21
  20.3 7.8 %collective-permute-start = (s32[128]{0:T(128)}, s32[128]{0:T(128)S(1)}, u32[]{:S(2)}, u32[]{:S(2)}) collective-permute-start(s32[128]{0:T(128)} %param.8), channel_id=1, source_target_pairs={{0,7},{1,0},{2,1},{3,2},{4,3},{5,4},{6,5},{7,6},{8,15},{9,8},{10,9... | collective-permute-start | bytes 1544 | tf_op jit(solution)/shard_map/ppermute | solution.py:21
  22.3 7.8 %collective-permute-start.3 = (s32[128]{0:T(128)}, s32[128]{0:T(128)S(1)}, u32[]{:S(2)}, u32[]{:S(2)}) collective-permute-start(s32[128]{0:T(128)} %param.8), channel_id=1, source_target_pairs={{0,1},{1,2},{2,3},{3,4},{4,5},{5,6},{6,7},{7,0},{8,9},{9,10},{10,1... | collective-permute-start | bytes 1544 | tf_op jit(solution)/shard_map/ppermute | solution.py:21
  28.2 7.1 %collective-permute-start.1 = (s32[128]{0:T(128)S(1)}, s32[128]{0:T(128)S(1)}, u32[]{:S(2)}, u32[]{:S(2)}) collective-permute-start(s32[128]{0:T(128)S(1)} %collective-permute-done), channel_id=1, source_target_pairs={{0,7},{1,0},{2,1},{3,2},{4,3},{5,4},{6,5},{7,6},{8,15},{9,8},{10,9... | collective-permute-start | bytes 1544 | tf_op jit(solution)/shard_map/ppermute | solution.py:21
  30.1 7.1 %collective-permute-start.4 = (s32[128]{0:T(128)S(1)}, s32[128]{0:T(128)S(1)}, u32[]{:S(2)}, u32[]{:S(2)}) collective-permute-start(s32[128]{0:T(128)S(1)} %collective-permute-done.3), channel_id=1, source_target_pairs={{0,1},{1,2},{2,3},{3,4},{4,5},{5,6},{6,7},{7,0},{8,9},{9,10},{10,1... | collective-permute-start | bytes 1544 | tf_op jit(solution)/shard_map/ppermute | solution.py:21
  35.3 72.9 %collective-permute-start.2 = (s32[128]{0:T(128)S(1)}, s32[128]{0:T(128)S(1)}, u32[]{:S(2)}, u32[]{:S(2)}) collective-permute-start(s32[128]{0:T(128)S(1)} %collective-permute-done.1), channel_id=1, source_target_pairs={{0,7},{1,0},{2,1},{3,2},{4,3},{5,4},{6,5},{7,6},{8,15},{9,8},{10,9... | collective-permute-start | bytes 1544 | tf_op jit(solution)/shard_map/ppermute | solution.py:21
  37.2 7.1 %collective-permute-start.5 = (s32[128]{0:T(128)S(1)}, s32[128]{0:T(128)S(1)}, u32[]{:S(2)}, u32[]{:S(2)}) collective-permute-start(s32[128]{0:T(128)S(1)} %collective-permute-done.4), channel_id=1, source_target_pairs={{0,1},{1,2},{2,3},{3,4},{4,5},{5,6},{6,7},{7,0},{8,9},{9,10},{10,1... | collective-permute-start | bytes 1544 | tf_op jit(solution)/shard_map/ppermute | solution.py:21
  42.3 69.3 %collective-permute-start.11 = (bf16[128,1600]{0,1:T(8,128)(2,1)}, bf16[128,1600]{0,1:T(8,128)(2,1)}, u32[]{:S(2)}, u32[]{:S(2)}) collective-permute-start(bf16[128,1600]{0,1:T(8,128)(2,1)} %collective-permute-done.10), channel_id=1, source_target_pairs={{0,1},{1,2},{2,3},{3,4},{4,5},{5,6},{6,7},{7,0},{8,9},{9,10},{10,1... | collective-permute-start | bytes 1228808 | tf_op jit(solution)/shard_map/ppermute | solution.py:21
  44.3 67.3 %collective-permute-start.6 = (s32[128]{0:T(128)S(1)}, s32[128]{0:T(128)S(1)}, u32[]{:S(2)}, u32[]{:S(2)}) collective-permute-start(s32[128]{0:T(128)S(1)} %collective-permute-done.5), channel_id=1, source_target_pairs={{0,1},{1,2},{2,3},{3,4},{4,5},{5,6},{6,7},{7,0},{8,9},{9,10},{10,1... | collective-permute-start | bytes 1544 | tf_op jit(solution)/shard_map/ppermute | solution.py:21
  106.0 39.9 %copy-start = (bf16[1024,1600]{1,0:T(8,128)(2,1)S(1)}, bf16[1024,1600]{1,0:T(8,128)(2,1)}, u32[]{:S(2)}) copy-start(bf16[1024,1600]{1,0:T(8,128)(2,1)} %all-gather.2.cloned.1.call-done) | copy-start | bytes 9830404
  106.0 46.2 %collective-permute-start.14 = (bf16[1024,1600]{0,1:T(8,128)(2,1)S(1)}, bf16[1024,1600]{0,1:T(8,128)(2,1)S(1)}, u32[]{:S(2)}, u32[]{:S(2)}) collective-permute-start(bf16[1024,1600]{0,1:T(8,128)(2,1)S(1)} %copy.9), channel_id=1, source_target_pairs={{0,8},{8,0},{1,9},{9,1},{2,10},{10,2},{3,11},{11,3},{4,12},{12,4},... | collective-permute-start | bytes 9830408 | tf_op jit(solution)/shard_map/ppermute | solution.py:21
  108.2 15.2 %collective-permute-start.8 = (bf16[128,1600]{0,1:T(8,128)(2,1)}, bf16[128,1600]{0,1:T(8,128)(2,1)S(1)}, u32[]{:S(2)}, u32[]{:S(2)}) collective-permute-start(bf16[128,1600]{0,1:T(8,128)(2,1)} %collective-permute-done.7), channel_id=1, source_target_pairs={{0,7},{1,0},{2,1},{3,2},{4,3},{5,4},{6,5},{7,6},{8,15},{9,8},{10,9... | collective-permute-start | bytes 1228808 | tf_op jit(solution)/shard_map/ppermute | solution.py:21
  111.6 15.8 %collective-permute-start.12 = (bf16[128,1600]{0,1:T(8,128)(2,1)}, bf16[128,1600]{0,1:T(8,128)(2,1)S(1)}, u32[]{:S(2)}, u32[]{:S(2)}) collective-permute-start(bf16[128,1600]{0,1:T(8,128)(2,1)} %collective-permute-done.11), channel_id=1, source_target_pairs={{0,1},{1,2},{2,3},{3,4},{4,5},{5,6},{6,7},{7,0},{8,9},{9,10},{10,1... | collective-permute-start | bytes 1228808 | tf_op jit(solution)/shard_map/ppermute | solution.py:21
  123.4 14.2 %collective-permute-start.9 = (bf16[128,1600]{0,1:T(8,128)(2,1)S(1)}, bf16[128,1600]{0,1:T(8,128)(2,1)S(1)}, u32[]{:S(2)}, u32[]{:S(2)}) collective-permute-start(bf16[128,1600]{0,1:T(8,128)(2,1)S(1)} %collective-permute-done.8), channel_id=1, source_target_pairs={{0,7},{1,0},{2,1},{3,2},{4,3},{5,4},{6,5},{7,6},{8,15},{9,8},{10,9... | collective-permute-start | bytes 1228808 | tf_op jit(solution)/shard_map/ppermute | solution.py:21
  127.4 13.2 %collective-permute-start.13 = (bf16[128,1600]{0,1:T(8,128)(2,1)S(1)}, bf16[128,1600]{0,1:T(8,128)(2,1)S(1)}, u32[]{:S(2)}, u32[]{:S(2)}) collective-permute-start(bf16[128,1600]{0,1:T(8,128)(2,1)S(1)} %collective-permute-done.12), channel_id=1, source_target_pairs={{0,1},{1,2},{2,3},{3,4},{4,5},{5,6},{6,7},{7,0},{8,9},{9,10},{10,1... | collective-permute-start | bytes 1228808 | tf_op jit(solution)/shard_map/ppermute | solution.py:21
  145.9 4.2 %copy-start.1 = (bf16[1024,1600]{0,1:T(8,128)(2,1)S(1)}, bf16[1024,1600]{0,1:T(8,128)(2,1)}, u32[]{:S(2)}) copy-start(bf16[1024,1600]{0,1:T(8,128)(2,1)} %constant_dynamic-update-slice_fusion.1) | copy-start | bytes 9830404
  156.5 38.2 %copy-start.2 = (s32[128]{0:T(128)S(1)}, s32[128]{0:T(128)}, u32[]{:S(2)}) copy-start(s32[128]{0:T(128)} %param.9) | copy-start | bytes 1540
  160.5 20.7 %collective-permute-start.15 = (f32[4,128]{1,0:T(4,128)S(1)}, f32[4,128]{1,0:T(4,128)S(1)}, u32[]{:S(2)}, u32[]{:S(2)}) collective-permute-start(f32[4,128]{1,0:T(4,128)S(1)} %bitcast.594), channel_id=1, source_target_pairs={{0,1},{1,2},{2,3},{3,4},{4,5},{5,6},{6,7},{7,0},{8,9},{9,10},{10,1... | collective-permute-start | bytes 6152 | tf_op jit(solution)/shard_map/ppermute | solution.py:21
  166.1 21.9 %collective-permute-start.18 = (f32[4,128]{1,0:T(4,128)S(1)}, f32[4,128]{1,0:T(4,128)S(1)}, u32[]{:S(2)}, u32[]{:S(2)}) collective-permute-start(f32[4,128]{1,0:T(4,128)S(1)} %bitcast.593), channel_id=1, source_target_pairs={{0,4},{1,5},{2,6},{3,7},{4,0},{5,1},{6,2},{7,3},{8,12},{9,13},{10,... | collective-permute-start | bytes 6152 | tf_op jit(solution)/shard_map/ppermute | solution.py:21
  171.2 18.8 %collective-permute-start.19 = (f32[4,128]{1,0:T(4,128)S(1)}, f32[4,128]{1,0:T(4,128)S(1)}, u32[]{:S(2)}, u32[]{:S(2)}) collective-permute-start(f32[4,128]{1,0:T(4,128)S(1)} %bitcast.592), channel_id=1, source_target_pairs={{0,5},{1,6},{2,7},{3,0},{4,1},{5,2},{6,3},{7,4},{8,13},{9,14},{10,... | collective-permute-start | bytes 6152 | tf_op jit(solution)/shard_map/ppermute | solution.py:21
  173.2 16.8 %collective-permute-start.20 = (f32[4,128]{1,0:T(4,128)S(1)}, f32[4,128]{1,0:T(4,128)S(1)}, u32[]{:S(2)}, u32[]{:S(2)}) collective-permute-start(f32[4,128]{1,0:T(4,128)S(1)} %bitcast.591), channel_id=1, source_target_pairs={{0,6},{1,7},{2,0},{3,1},{4,2},{5,3},{6,4},{7,5},{8,14},{9,15},{10,... | collective-permute-start | bytes 6152 | tf_op jit(solution)/shard_map/ppermute | solution.py:21
  176.1 13.9 %collective-permute-start.16 = (f32[4,128]{1,0:T(4,128)S(1)}, f32[4,128]{1,0:T(4,128)S(1)}, u32[]{:S(2)}, u32[]{:S(2)}) collective-permute-start(f32[4,128]{1,0:T(4,128)S(1)} %bitcast.597), channel_id=1, source_target_pairs={{0,2},{1,3},{2,4},{3,5},{4,6},{5,7},{6,0},{7,1},{8,10},{9,11},{10,... | collective-permute-start | bytes 6152 | tf_op jit(solution)/shard_map/ppermute | solution.py:21
  181.2 8.8 %collective-permute-start.17 = (f32[4,128]{1,0:T(4,128)S(1)}, f32[4,128]{1,0:T(4,128)S(1)}, u32[]{:S(2)}, u32[]{:S(2)}) collective-permute-start(f32[4,128]{1,0:T(4,128)S(1)} %bitcast.596), channel_id=1, source_target_pairs={{0,3},{1,4},{2,5},{3,6},{4,7},{5,0},{6,1},{7,2},{8,11},{9,12},{10,... | collective-permute-start | bytes 6152 | tf_op jit(solution)/shard_map/ppermute | solution.py:21
  188.0 6.7 %collective-permute-start.21 = (f32[4,128]{1,0:T(4,128)S(1)}, f32[4,128]{1,0:T(4,128)S(1)}, u32[]{:S(2)}, u32[]{:S(2)}) collective-permute-start(f32[4,128]{1,0:T(4,128)S(1)} %bitcast.595), channel_id=1, source_target_pairs={{0,7},{1,0},{2,1},{3,2},{4,3},{5,4},{6,5},{7,6},{8,15},{9,8},{10,9... | collective-permute-start | bytes 6152 | tf_op jit(solution)/shard_map/ppermute | solution.py:21
Sparse Core Ops, SparseCore 0:
  11.2 90.4 all-gather.1
where the time goes:
time: 204 us; the launch traced here: 203 us
  starting transfers between devices  82.5 us (40%)
  waiting for transfers between devices  72.8 us (36%)
  between operations  14.5 us (7%)
  local copies, waits for them, and re-layouts  13.7 us (7%)
  matrix products  10.6 us (5%)
  other arithmetic  8.53 us (4%)
    ppermute x22, starting transfers between devices, shift(): lax.ppermute(value, axis, [(i, (i + step) % size) for i in range(size)])  82.4 us
    all_gather x1, waiting for transfers between devices, on_device(): half = lax.all_gather(unembed, ('z', 'x'), axis=0, tiled=True)  52.7 us
    ppermute x22, waiting for transfers between devices, shift(): lax.ppermute(value, axis, [(i, (i + step) % size) for i in range(size)])  19.5 us
    dot_general x4, matrix products, chunk_stats(): lax.dot_general(normed, piece, (((1,), (1,)), ((), ())), preferred_elemen...  10.6 us
    unnamed x19, local copies, waits for them, and re-layouts  7.66 us
    all_gather x1, local copies, waits for them, and re-layouts, on_device(): half = lax.all_gather(unembed, ('z', 'x'), axis=0, tiled=True)  4.26 us
  transfers between devices with their start and end apart: 23, of which 5 were waited for; matrix products, arithmetic and copies ran while one was open for 12% of the time, Pallas kernels for 0%

commit v1 on v0

--- a/solution.py
+++ b/solution.py
@@ -56,7 +56,8 @@
         blocks[d] = cur
     rows = jnp.concatenate([b[0] for b in blocks], axis=0)
     wanted = jnp.concatenate([b[1] for b in blocks], axis=0)
-    half = lax.all_gather(unembed, ("z", "x"), axis=0, tiled=True)
+    repeated = jnp.stack([unembed] * lax.axis_size(("z", "x")))
+    half = jnp.concatenate(lax.all_to_all(repeated, ("z", "x"), 0, 0), axis=0)
     other = shift(half, "c", nc, 1)
 
     def ids_of(core):

time: 204 us -> 173 us (0.85)
  waiting for transfers between devices: 72.8 us -> 45.1 us
  between operations: 14.5 us -> 1.13 us
  local copies, waits for them, and re-layouts: 13.7 us -> 20.2 us
  starting transfers between devices: 82.5 us -> 88.5 us
  matrix products: 10.6 us -> 8.53 us
    all_gather x1 -> x0, waiting for transfers between devices: 52.7 us -> none  [on_device(): half = lax.all_gather(unembed, ('z', 'x'), axis=0, tiled=True)]
    all_to_all x0 -> x1, waiting for transfers between devices: none -> 25.8 us  [on_device(): half = jnp.concatenate(lax.all_to_all(repeated, ('z', 'x'), 0, 0), axis=0)]
    all_to_all x0 -> x1, starting transfers between devices: none -> 13.3 us  [on_device(): half = jnp.concatenate(lax.all_to_all(repeated, ('z', 'x'), 0, 0), axis=0)]
    ppermute x22, starting transfers between devices: 82.4 us -> 75.2 us  [shift(): lax.ppermute(value, axis, [(i, (i + step) % size) for i in range(size)])]
    all_gather x1 -> x0, local copies, waits for them, and re-layouts: 4.26 us -> none  [on_device(): half = lax.all_gather(unembed, ('z', 'x'), axis=0, tiled=True)]
    unnamed x19 -> x21, local copies, waits for them, and re-layouts: 7.66 us -> 11.7 us
    reshape x0 -> x1, local copies, waits for them, and re-layouts: none -> 3.59 us  [on_device(): half = jnp.concatenate(lax.all_to_all(repeated, ('z', 'x'), 0, 0), axis=0)]
    another operation x0 -> x1, local copies, waits for them, and re-layouts: none -> 2.85 us  [on_device(): repeated = jnp.stack([unembed] * lax.axis_size(('z', 'x')))]
  transfers between devices with their start and end apart: 23 -> 23, of which waited for: 5 -> 6; matrix products, arithmetic and copies ran while one was open for 12% -> 14% of each run, Pallas kernels for 0% -> 0%
where the time goes in v1:
time: 173 us; the launch traced here: 172 us
  starting transfers between devices  88.5 us (51%)
  waiting for transfers between devices  45.1 us (26%)
  local copies, waits for them, and re-layouts  20.2 us (12%)
  matrix products  8.53 us (5%)
  other arithmetic  8.45 us (5%)
    ppermute x22, starting transfers between devices, shift(): lax.ppermute(value, axis, [(i, (i + step) % size) for i in range(size)])  75.2 us
    all_to_all x1, waiting for transfers between devices, on_device(): half = jnp.concatenate(lax.all_to_all(repeated, ('z', 'x'), 0, 0), axis=0)  25.8 us
    ppermute x22, waiting for transfers between devices, shift(): lax.ppermute(value, axis, [(i, (i + step) % size) for i in range(size)])  19.3 us
    all_to_all x1, starting transfers between devices, on_device(): half = jnp.concatenate(lax.all_to_all(repeated, ('z', 'x'), 0, 0), axis=0)  13.3 us
    unnamed x21, local copies, waits for them, and re-layouts  11.7 us
    dot_general x4, matrix products, chunk_stats(): lax.dot_general(normed, piece, (((1,), (1,)), ((), ())), preferred_elemen...  8.53 us
    reduce_sum x1, other arithmetic, chunk_stats(): jnp.sum(weights, axis=1)  3.86 us
    reshape x1, local copies, waits for them, and re-layouts, on_device(): half = jnp.concatenate(lax.all_to_all(repeated, ('z', 'x'), 0, 0), axis=0)  3.59 us
  transfers between devices with their start and end apart: 23, of which 6 were waited for; matrix products, arithmetic and copies ran while one was open for 14% of the time, Pallas kernels for 0%

profile of v1, /device:TPU:56, one launch (start us, length us, event | category | flops | bytes accessed | tf_op | source)
XLA Modules:
  0.0 171.9 jit_solution(12324356503250392202)
XLA Ops:
  0.6 2.9 %stack.4 = bf16[32,32,1600]{2,1,0:T(8,128)(2,1)} broadcast(bf16[32,1600]{1,0:T(8,128)(2,1)} %param.7), dimensions={1,2} | broadcast | bytes 3379200 | tf_op jit(solution)/shard_map/stack | solution.py:59
  3.5 13.3 %all-to-all-start = ((bf16[32,32,1600]{2,1,0:T(8,128)(2,1)}), bf16[32,32,1600]{2,1,0:T(8,128)(2,1)S(1)}, u32[]{:S(2)}, u32[]{:S(2)}) async-start(bf16[32,32,1600]{2,1,0:T(8,128)(2,1)} %stack.4), calls=%async_computation | async-start | bytes 6815744 | tf_op jit(solution)/shard_map/all_to_all | solution.py:60
  16.8 1.2 fusion.8
  18.0 2.2 %constant_dynamic-update-slice_fusion.8 = (bf16[1024,1600]{0,1:T(8,128)(2,1)}, bf16[128,1600]{0,1:T(8,128)(2,1)}) fusion(f32[1600]{0:T(1024)S(1)} %copy-done.1, f32[128]{0:T(128)S(1)} %add_rsqrt_fusion, bf16[128,1600]{0,1:T(8,128)(2,1)} %param.5), kind=kLoop, calls=%fused_computation.33 | loop fusion | flops 819199 | bytes 1235712
  20.2 3.2 %collective-permute-start.7 = (bf16[128,1600]{0,1:T(8,128)(2,1)}, bf16[128,1600]{0,1:T(8,128)(2,1)}, u32[]{:S(2)}, u32[]{:S(2)}) collective-permute-start(bf16[128,1600]{0,1:T(8,128)(2,1)} %get-tuple-element.18), channel_id=1, source_target_pairs={{0,7},{1,0},{2,1},{3,2},{4,3},{5,4},{6,5},{7,6},{8,15},{9,8},{10,9... | collective-permute-start | bytes 1228808 | tf_op jit(solution)/shard_map/ppermute | solution.py:21
  23.5 3.8 %collective-permute-start.10 = (bf16[128,1600]{0,1:T(8,128)(2,1)}, bf16[128,1600]{0,1:T(8,128)(2,1)}, u32[]{:S(2)}, u32[]{:S(2)}) collective-permute-start(bf16[128,1600]{0,1:T(8,128)(2,1)} %get-tuple-element.18), channel_id=1, source_target_pairs={{0,1},{1,2},{2,3},{3,4},{4,5},{5,6},{6,7},{7,0},{8,9},{9,10},{10,1... | collective-permute-start | bytes 1228808 | tf_op jit(solution)/shard_map/ppermute | solution.py:21
  27.3 2.0 %collective-permute-start = (s32[128]{0:T(128)S(1)}, s32[128]{0:T(128)S(1)}, u32[]{:S(2)}, u32[]{:S(2)}) collective-permute-start(s32[128]{0:T(128)S(1)} %copy-done.3), channel_id=1, source_target_pairs={{0,7},{1,0},{2,1},{3,2},{4,3},{5,4},{6,5},{7,6},{8,15},{9,8},{10,9... | collective-permute-start | bytes 1544 | tf_op jit(solution)/shard_map/ppermute | solution.py:21
  29.4 5.0 %collective-permute-start.3 = (s32[128]{0:T(128)S(1)}, s32[128]{0:T(128)S(1)}, u32[]{:S(2)}, u32[]{:S(2)}) collective-permute-start(s32[128]{0:T(128)S(1)} %copy-done.3), channel_id=1, source_target_pairs={{0,1},{1,2},{2,3},{3,4},{4,5},{5,6},{6,7},{7,0},{8,9},{9,10},{10,1... | collective-permute-start | bytes 1544 | tf_op jit(solution)/shard_map/ppermute | solution.py:21
  34.6 2.0 %collective-permute-start.1 = (s32[128]{0:T(128)S(1)}, s32[128]{0:T(128)S(1)}, u32[]{:S(2)}, u32[]{:S(2)}) collective-permute-start(s32[128]{0:T(128)S(1)} %collective-permute-done), channel_id=1, source_target_pairs={{0,7},{1,0},{2,1},{3,2},{4,3},{5,4},{6,5},{7,6},{8,15},{9,8},{10,9... | collective-permute-start | bytes 1544 | tf_op jit(solution)/shard_map/ppermute | solution.py:21
  36.6 5.0 %collective-permute-start.4 = (s32[128]{0:T(128)S(1)}, s32[128]{0:T(128)S(1)}, u32[]{:S(2)}, u32[]{:S(2)}) collective-permute-start(s32[128]{0:T(128)S(1)} %collective-permute-done.3), channel_id=1, source_target_pairs={{0,1},{1,2},{2,3},{3,4},{4,5},{5,6},{6,7},{7,0},{8,9},{9,10},{10,1... | collective-permute-start | bytes 1544 | tf_op jit(solution)/shard_map/ppermute | solution.py:21
  41.7 1.9 %collective-permute-start.2 = (s32[128]{0:T(128)S(1)}, s32[128]{0:T(128)S(1)}, u32[]{:S(2)}, u32[]{:S(2)}) collective-permute-start(s32[128]{0:T(128)S(1)} %collective-permute-done.1), channel_id=1, source_target_pairs={{0,7},{1,0},{2,1},{3,2},{4,3},{5,4},{6,5},{7,6},{8,15},{9,8},{10,9... | collective-permute-start | bytes 1544 | tf_op jit(solution)/shard_map/ppermute | solution.py:21
  43.6 5.1 %collective-permute-start.5 = (s32[128]{0:T(128)S(1)}, s32[128]{0:T(128)S(1)}, u32[]{:S(2)}, u32[]{:S(2)}) collective-permute-start(s32[128]{0:T(128)S(1)} %collective-permute-done.4), channel_id=1, source_target_pairs={{0,1},{1,2},{2,3},{3,4},{4,5},{5,6},{6,7},{7,0},{8,9},{9,10},{10,1... | collective-permute-start | bytes 1544 | tf_op jit(solution)/shard_map/ppermute | solution.py:21
  48.8 1.9 %collective-permute-start.11 = (bf16[128,1600]{0,1:T(8,128)(2,1)}, bf16[128,1600]{0,1:T(8,128)(2,1)}, u32[]{:S(2)}, u32[]{:S(2)}) collective-permute-start(bf16[128,1600]{0,1:T(8,128)(2,1)} %collective-permute-done.10), channel_id=1, source_target_pairs={{0,1},{1,2},{2,3},{3,4},{4,5},{5,6},{6,7},{7,0},{8,9},{9,10},{10,1... | collective-permute-start | bytes 1228808 | tf_op jit(solution)/shard_map/ppermute | solution.py:21
  50.7 4.7 %collective-permute-start.6 = (s32[128]{0:T(128)S(1)}, s32[128]{0:T(128)S(1)}, u32[]{:S(2)}, u32[]{:S(2)}) collective-permute-start(s32[128]{0:T(128)S(1)} %collective-permute-done.5), channel_id=1, source_target_pairs={{0,1},{1,2},{2,3},{3,4},{4,5},{5,6},{6,7},{7,0},{8,9},{9,10},{10,1... | collective-permute-start | bytes 1544 | tf_op jit(solution)/shard_map/ppermute | solution.py:21
  55.4 1.9 %collective-permute-start.8 = (bf16[128,1600]{0,1:T(8,128)(2,1)}, bf16[128,1600]{0,1:T(8,128)(2,1)}, u32[]{:S(2)}, u32[]{:S(2)}) collective-permute-start(bf16[128,1600]{0,1:T(8,128)(2,1)} %collective-permute-done.7), channel_id=1, source_target_pairs={{0,7},{1,0},{2,1},{3,2},{4,3},{5,4},{6,5},{7,6},{8,15},{9,8},{10,9... | collective-permute-start | bytes 1228808 | tf_op jit(solution)/shard_map/ppermute | solution.py:21
  57.3 2.5 %collective-permute-done.6 = s32[128]{0:T(128)S(1)} collective-permute-done((s32[128]{0:T(128)S(1)}, s32[128]{0:T(128)S(1)}, u32[]{:S(2)}, u32[]{:S(2)}) %collective-permute-start.6) | collective-permute-done | bytes 544 | tf_op jit(solution)/shard_map/ppermute | solution.py:21
  59.9 3.4 %collective-permute-start.12 = (bf16[128,1600]{0,1:T(8,128)(2,1)}, bf16[128,1600]{0,1:T(8,128)(2,1)}, u32[]{:S(2)}, u32[]{:S(2)}) collective-permute-start(bf16[128,1600]{0,1:T(8,128)(2,1)} %collective-permute-done.11), channel_id=1, source_target_pairs={{0,1},{1,2},{2,3},{3,4},{4,5},{5,6},{6,7},{7,0},{8,9},{9,10},{10,1... | collective-permute-start | bytes 1228808 | tf_op jit(solution)/shard_map/ppermute | solution.py:21
  63.3 3.5 %collective-permute-done.8 = bf16[128,1600]{0,1:T(8,128)(2,1)} collective-permute-done((bf16[128,1600]{0,1:T(8,128)(2,1)}, bf16[128,1600]{0,1:T(8,128)(2,1)}, u32[]{:S(2)}, u32[]{:S(2)}) %collective-permute-start.8) | collective-permute-done | bytes 409632 | tf_op jit(solution)/shard_map/ppermute | solution.py:21
  66.9 1.9 %collective-permute-start.9 = (bf16[128,1600]{0,1:T(8,128)(2,1)}, bf16[128,1600]{0,1:T(8,128)(2,1)}, u32[]{:S(2)}, u32[]{:S(2)}) collective-permute-start(bf16[128,1600]{0,1:T(8,128)(2,1)} %collective-permute-done.8), channel_id=1, source_target_pairs={{0,7},{1,0},{2,1},{3,2},{4,3},{5,4},{6,5},{7,6},{8,15},{9,8},{10,9... | collective-permute-start | bytes 1228808 | tf_op jit(solution)/shard_map/ppermute | solution.py:21
  68.8 25.8 %all-to-all-done = bf16[32,32,1600]{2,1,0:T(8,128)(2,1)S(1)} async-done(((bf16[32,32,1600]{2,1,0:T(8,128)(2,1)}), bf16[32,32,1600]{2,1,0:T(8,128)(2,1)S(1)}, u32[]{:S(2)}, u32[]{:S(2)}) %all-to-all-start) | async-done | bytes 3276832 | tf_op jit(solution)/shard_map/all_to_all | solution.py:60
  94.6 3.6 %copy.9 = bf16[1024,1600]{0,1:T(8,128)(2,1)} copy(bf16[1024,1600]{1,0:T(8,128)(2,1)S(1)} %bitcast.596) | data formatting | bytes 6553600 | tf_op jit(solution)/shard_map/reshape | solution.py:60
  98.2 1.9 %collective-permute-start.14 = (bf16[1024,1600]{0,1:T(8,128)(2,1)}, bf16[1024,1600]{0,1:T(8,128)(2,1)S(1)}, u32[]{:S(2)}, u32[]{:S(2)}) collective-permute-start(bf16[1024,1600]{0,1:T(8,128)(2,1)} %copy.9), channel_id=1, source_target_pairs={{0,8},{8,0},{1,9},{9,1},{2,10},{10,2},{3,11},{11,3},{4,12},{12,4},... | collective-permute-start | bytes 9830408 | tf_op jit(solution)/shard_map/ppermute | solution.py:21
  100.1 1.8 %constant_dynamic-update-slice_fusion.7 = bf16[1024,1600]{0,1:T(8,128)(2,1)} fusion(bf16[1024,1600]{0,1:T(8,128)(2,1)} %get-tuple-element.17, bf16[128,1600]{0,1:T(8,128)(2,1)} %collective-permute-done.7), kind=kLoop, calls=%fused_computation.32 | loop fusion | bytes 819200
  102.0 1.9 %collective-permute-start.13 = (bf16[128,1600]{0,1:T(8,128)(2,1)}, bf16[128,1600]{0,1:T(8,128)(2,1)S(1)}, u32[]{:S(2)}, u32[]{:S(2)}) collective-permute-start(bf16[128,1600]{0,1:T(8,128)(2,1)} %collective-permute-done.12), channel_id=1, source_target_pairs={{0,1},{1,2},{2,3},{3,4},{4,5},{5,6},{6,7},{7,0},{8,9},{9,10},{10,1... | collective-permute-start | bytes 1228808 | tf_op jit(solution)/shard_map/ppermute | solution.py:21
  103.9 1.8 %constant_dynamic-update-slice_fusion.6 = bf16[1024,1600]{0,1:T(8,128)(2,1)} fusion(bf16[1024,1600]{0,1:T(8,128)(2,1)} %constant_dynamic-update-slice_fusion.7, bf16[128,1600]{0,1:T(8,128)(2,1)} %collective-permute-done.8), kind=kLoop, calls=%fused_computation.31 | loop fusion | bytes 819200
  105.7 1.8 %constant_dynamic-update-slice_fusion.5 = bf16[1024,1600]{0,1:T(8,128)(2,1)} fusion(bf16[1024,1600]{0,1:T(8,128)(2,1)} %constant_dynamic-update-slice_fusion.6, bf16[128,1600]{0,1:T(8,128)(2,1)} %collective-permute-done.9), kind=kLoop, calls=%fused_computation.30 | loop fusion | bytes 819200
  107.5 8.4 %collective-permute-done.13 = bf16[128,1600]{0,1:T(8,128)(2,1)S(1)} collective-permute-done((bf16[128,1600]{0,1:T(8,128)(2,1)}, bf16[128,1600]{0,1:T(8,128)(2,1)S(1)}, u32[]{:S(2)}, u32[]{:S(2)}) %collective-permute-start.13) | collective-permute-done | bytes 409632 | tf_op jit(solution)/shard_map/ppermute | solution.py:21
  115.9 0.8 constant_dynamic-update-slice_fusion.4
  116.7 1.8 %constant_dynamic-update-slice_fusion.3 = bf16[1024,1600]{0,1:T(8,128)(2,1)} fusion(bf16[1024,1600]{0,1:T(8,128)(2,1)} %constant_dynamic-update-slice_fusion.4, bf16[128,1600]{0,1:T(8,128)(2,1)} %collective-permute-done.12), kind=kLoop, calls=%fused_computation.28 | loop fusion | bytes 819200
  118.6 1.8 %constant_dynamic-update-slice_fusion.2 = bf16[1024,1600]{0,1:T(8,128)(2,1)} fusion(bf16[1024,1600]{0,1:T(8,128)(2,1)} %constant_dynamic-update-slice_fusion.3, bf16[128,1600]{0,1:T(8,128)(2,1)} %collective-permute-done.11), kind=kLoop, calls=%fused_computation.27 | loop fusion | bytes 819200
  120.4 1.8 %constant_dynamic-update-slice_fusion.1 = bf16[1024,1600]{0,1:T(8,128)(2,1)} fusion(bf16[1024,1600]{0,1:T(8,128)(2,1)} %constant_dynamic-update-slice_fusion.2, bf16[128,1600]{0,1:T(8,128)(2,1)} %collective-permute-done.10), kind=kLoop, calls=%fused_computation.26 | loop fusion | bytes 819200 | tf_op jit(solution)/shard_map/concatenate | solution.py:57
  122.2 0.3 fusion.81
  122.5 1.6 copy-done
  124.1 2.1 %fusion.87 = (f32[1024]{0:T(1024)S(1)}, f32[1024,512]{0,1:T(8,128)S(1)}) fusion(bf16[512,1600]{1,0:T(8,128)(2,1)S(1)} %bitcast.598, bf16[1024,1600]{0,1:T(8,128)(2,1)S(1)} %copy-done), kind=kOutput, calls=%fused_computation.198 | convolution fusion | flops 1678244864 | bytes 7016448 | tf_op jit(solution)/shard_map/dot_general | solution.py:25
  126.2 2.1 %fusion.84 = (f32[1024]{0:T(1024)S(1)}, f32[1024,512]{0,1:T(8,128)S(1)}) fusion(bf16[512,1600]{1,0:T(8,128)(2,1)S(1)} %bitcast.597, bf16[1024,1600]{0,1:T(8,128)(2,1)S(1)} %copy-done), kind=kOutput, calls=%fused_computation.195 | convolution fusion | flops 1678244864 | bytes 7016448 | tf_op jit(solution)/shard_map/dot_general | solution.py:25
  128.4 2.1 %fusion.86 = (f32[1024]{0:T(1024)S(1)}, f32[1024,512]{0,1:T(8,128)S(1)}) fusion(bf16[1024,1600]{0,1:T(8,128)(2,1)S(1)} %copy-done, bf16[1024,1600]{0,1:T(8,128)(2,1)S(1)} %collective-permute-done.14), kind=kOutput, calls=%fused_computation.197 | convolution fusion | flops 1678244864 | bytes 7016448 | tf_op jit(solution)/shard_map/dot_general | solution.py:25
  130.5 2.1 %fusion.85 = (f32[1024]{0:T(1024)S(1)}, f32[1024,512]{0,1:T(8,128)S(1)}) fusion(bf16[1024,1600]{0,1:T(8,128)(2,1)S(1)} %copy-done, bf16[1024,1600]{0,1:T(8,128)(2,1)S(1)} %collective-permute-done.14), kind=kOutput, calls=%fused_computation.196 | convolution fusion | flops 1678244864 | bytes 7016448 | tf_op jit(solution)/shard_map/dot_general | solution.py:25
  132.7 3.9 %exponential_reduce_fusion.2 = (f32[1024]{0:T(1024)S(1)}, f32[1024]{0:T(1024)S(1)}, f32[1024]{0:T(1024)S(1)}, f32[1024]{0:T(1024)S(1)}, f32[1024]{0:T(1024)S(1)}...) fusion(f32[1024,512]{0,1:T(8,128)S(1)} %get-tuple-element.45, ...), kind=kLoop, calls=%fused_computation.5 | loop fusion | flops 14667776 | bytes 8466432 | tf_op jit(solution)/shard_map/reduce_sum | solution.py:32
  136.6 3.4 %collective-permute-start.15 = (f32[4,128]{1,0:T(4,128)S(1)}, f32[4,128]{1,0:T(4,128)S(1)}, u32[]{:S(2)}, u32[]{:S(2)}) collective-permute-start(f32[4,128]{1,0:T(4,128)S(1)} %bitcast.602), channel_id=1, source_target_pairs={{0,1},{1,2},{2,3},{3,4},{4,5},{5,6},{6,7},{7,0},{8,9},{9,10},{10,1... | collective-permute-start | bytes 6152 | tf_op jit(solution)/shard_map/ppermute | solution.py:21
  140.1 7.2 %collective-permute-start.18 = (f32[4,128]{1,0:T(4,128)S(1)}, f32[4,128]{1,0:T(4,128)S(1)}, u32[]{:S(2)}, u32[]{:S(2)}) collective-permute-start(f32[4,128]{1,0:T(4,128)S(1)} %bitcast.601), channel_id=1, source_target_pairs={{0,4},{1,5},{2,6},{3,7},{4,0},{5,1},{6,2},{7,3},{8,12},{9,13},{10,... | collective-permute-start | bytes 6152 | tf_op jit(solution)/shard_map/ppermute | solution.py:21
  147.3 1.9 %collective-permute-start.19 = (f32[4,128]{1,0:T(4,128)S(1)}, f32[4,128]{1,0:T(4,128)S(1)}, u32[]{:S(2)}, u32[]{:S(2)}) collective-permute-start(f32[4,128]{1,0:T(4,128)S(1)} %bitcast.600), channel_id=1, source_target_pairs={{0,5},{1,6},{2,7},{3,0},{4,1},{5,2},{6,3},{7,4},{8,13},{9,14},{10,... | collective-permute-start | bytes 6152 | tf_op jit(solution)/shard_map/ppermute | solution.py:21
  149.2 3.1 %collective-permute-start.20 = (f32[4,128]{1,0:T(4,128)S(1)}, f32[4,128]{1,0:T(4,128)S(1)}, u32[]{:S(2)}, u32[]{:S(2)}) collective-permute-start(f32[4,128]{1,0:T(4,128)S(1)} %bitcast.599), channel_id=1, source_target_pairs={{0,6},{1,7},{2,0},{3,1},{4,2},{5,3},{6,4},{7,5},{8,14},{9,15},{10,... | collective-permute-start | bytes 6152 | tf_op jit(solution)/shard_map/ppermute | solution.py:21
  152.3 4.9 %collective-permute-start.16 = (f32[4,128]{1,0:T(4,128)S(1)}, f32[4,128]{1,0:T(4,128)S(1)}, u32[]{:S(2)}, u32[]{:S(2)}) collective-permute-start(f32[4,128]{1,0:T(4,128)S(1)} %bitcast.605), channel_id=1, source_target_pairs={{0,2},{1,3},{2,4},{3,5},{4,6},{5,7},{6,0},{7,1},{8,10},{9,11},{10,... | collective-permute-start | bytes 6152 | tf_op jit(solution)/shard_map/ppermute | solution.py:21
  157.2 6.9 %collective-permute-start.17 = (f32[4,128]{1,0:T(4,128)S(1)}, f32[4,128]{1,0:T(4,128)S(1)}, u32[]{:S(2)}, u32[]{:S(2)}) collective-permute-start(f32[4,128]{1,0:T(4,128)S(1)} %bitcast.604), channel_id=1, source_target_pairs={{0,3},{1,4},{2,5},{3,6},{4,7},{5,0},{6,1},{7,2},{8,11},{9,12},{10,... | collective-permute-start | bytes 6152 | tf_op jit(solution)/shard_map/ppermute | solution.py:21
  164.1 1.9 %collective-permute-start.21 = (f32[4,128]{1,0:T(4,128)S(1)}, f32[4,128]{1,0:T(4,128)S(1)}, u32[]{:S(2)}, u32[]{:S(2)}) collective-permute-start(f32[4,128]{1,0:T(4,128)S(1)} %bitcast.603), channel_id=1, source_target_pairs={{0,7},{1,0},{2,1},{3,2},{4,3},{5,4},{6,5},{7,6},{8,15},{9,8},{10,9... | collective-permute-start | bytes 6152 | tf_op jit(solution)/shard_map/ppermute | solution.py:21
  166.1 4.7 %collective-permute-done.21 = f32[4,128]{1,0:T(4,128)S(1)} collective-permute-done((f32[4,128]{1,0:T(4,128)S(1)}, f32[4,128]{1,0:T(4,128)S(1)}, u32[]{:S(2)}, u32[]{:S(2)}) %collective-permute-start.21) | collective-permute-done | bytes 2080 | tf_op jit(solution)/shard_map/ppermute | solution.py:21
  170.8 0.5 subtract_multiply_fusion
  171.4 0.5 fusion.78
  (42 shorter events, 0.3 us)
Async XLA Ops:
  3.5 14.5 %copy-start.1 = (f32[1600]{0:T(1024)S(1)}, f32[1600]{0:T(1024)}, u32[]{:S(2)}) copy-start(f32[1600]{0:T(1024)} %param.6) | copy-start | bytes 19204
  3.5 23.8 %copy-start.3 = (s32[128]{0:T(128)S(1)}, s32[128]{0:T(128)}, u32[]{:S(2)}) copy-start(s32[128]{0:T(128)} %param.8) | copy-start | bytes 1540
  3.5 91.1 %all-to-all-start = ((bf16[32,32,1600]{2,1,0:T(8,128)(2,1)}), bf16[32,32,1600]{2,1,0:T(8,128)(2,1)S(1)}, u32[]{:S(2)}, u32[]{:S(2)}) async-start(bf16[32,32,1600]{2,1,0:T(8,128)(2,1)} %stack.4), calls=%async_computation | async-start | bytes 6815744 | tf_op jit(solution)/shard_map/all_to_all | solution.py:60
  20.2 35.2 %collective-permute-start.7 = (bf16[128,1600]{0,1:T(8,128)(2,1)}, bf16[128,1600]{0,1:T(8,128)(2,1)}, u32[]{:S(2)}, u32[]{:S(2)}) collective-permute-start(bf16[128,1600]{0,1:T(8,128)(2,1)} %get-tuple-element.18), channel_id=1, source_target_pairs={{0,7},{1,0},{2,1},{3,2},{4,3},{5,4},{6,5},{7,6},{8,15},{9,8},{10,9... | collective-permute-start | bytes 1228808 | tf_op jit(solution)/shard_map/ppermute | solution.py:21
  23.5 25.3 %collective-permute-start.10 = (bf16[128,1600]{0,1:T(8,128)(2,1)}, bf16[128,1600]{0,1:T(8,128)(2,1)}, u32[]{:S(2)}, u32[]{:S(2)}) collective-permute-start(bf16[128,1600]{0,1:T(8,128)(2,1)} %get-tuple-element.18), channel_id=1, source_target_pairs={{0,1},{1,2},{2,3},{3,4},{4,5},{5,6},{6,7},{7,0},{8,9},{9,10},{10,1... | collective-permute-start | bytes 1228808 | tf_op jit(solution)/shard_map/ppermute | solution.py:21
  27.3 7.3 %collective-permute-start = (s32[128]{0:T(128)S(1)}, s32[128]{0:T(128)S(1)}, u32[]{:S(2)}, u32[]{:S(2)}) collective-permute-start(s32[128]{0:T(128)S(1)} %copy-done.3), channel_id=1, source_target_pairs={{0,7},{1,0},{2,1},{3,2},{4,3},{5,4},{6,5},{7,6},{8,15},{9,8},{10,9... | collective-permute-start | bytes 1544 | tf_op jit(solution)/shard_map/ppermute | solution.py:21
  29.4 7.3 %collective-permute-start.3 = (s32[128]{0:T(128)S(1)}, s32[128]{0:T(128)S(1)}, u32[]{:S(2)}, u32[]{:S(2)}) collective-permute-start(s32[128]{0:T(128)S(1)} %copy-done.3), channel_id=1, source_target_pairs={{0,1},{1,2},{2,3},{3,4},{4,5},{5,6},{6,7},{7,0},{8,9},{9,10},{10,1... | collective-permute-start | bytes 1544 | tf_op jit(solution)/shard_map/ppermute | solution.py:21
  34.6 7.1 %collective-permute-start.1 = (s32[128]{0:T(128)S(1)}, s32[128]{0:T(128)S(1)}, u32[]{:S(2)}, u32[]{:S(2)}) collective-permute-start(s32[128]{0:T(128)S(1)} %collective-permute-done), channel_id=1, source_target_pairs={{0,7},{1,0},{2,1},{3,2},{4,3},{5,4},{6,5},{7,6},{8,15},{9,8},{10,9... | collective-permute-start | bytes 1544 | tf_op jit(solution)/shard_map/ppermute | solution.py:21
  36.6 7.0 %collective-permute-start.4 = (s32[128]{0:T(128)S(1)}, s32[128]{0:T(128)S(1)}, u32[]{:S(2)}, u32[]{:S(2)}) collective-permute-start(s32[128]{0:T(128)S(1)} %collective-permute-done.3), channel_id=1, source_target_pairs={{0,1},{1,2},{2,3},{3,4},{4,5},{5,6},{6,7},{7,0},{8,9},{9,10},{10,1... | collective-permute-start | bytes 1544 | tf_op jit(solution)/shard_map/ppermute | solution.py:21
  41.7 13.7 %collective-permute-start.2 = (s32[128]{0:T(128)S(1)}, s32[128]{0:T(128)S(1)}, u32[]{:S(2)}, u32[]{:S(2)}) collective-permute-start(s32[128]{0:T(128)S(1)} %collective-permute-done.1), channel_id=1, source_target_pairs={{0,7},{1,0},{2,1},{3,2},{4,3},{5,4},{6,5},{7,6},{8,15},{9,8},{10,9... | collective-permute-start | bytes 1544 | tf_op jit(solution)/shard_map/ppermute | solution.py:21
  43.6 7.1 %collective-permute-start.5 = (s32[128]{0:T(128)S(1)}, s32[128]{0:T(128)S(1)}, u32[]{:S(2)}, u32[]{:S(2)}) collective-permute-start(s32[128]{0:T(128)S(1)} %collective-permute-done.4), channel_id=1, source_target_pairs={{0,1},{1,2},{2,3},{3,4},{4,5},{5,6},{6,7},{7,0},{8,9},{9,10},{10,1... | collective-permute-start | bytes 1544 | tf_op jit(solution)/shard_map/ppermute | solution.py:21
  48.8 11.1 %collective-permute-start.11 = (bf16[128,1600]{0,1:T(8,128)(2,1)}, bf16[128,1600]{0,1:T(8,128)(2,1)}, u32[]{:S(2)}, u32[]{:S(2)}) collective-permute-start(bf16[128,1600]{0,1:T(8,128)(2,1)} %collective-permute-done.10), channel_id=1, source_target_pairs={{0,1},{1,2},{2,3},{3,4},{4,5},{5,6},{6,7},{7,0},{8,9},{9,10},{10,1... | collective-permute-start | bytes 1228808 | tf_op jit(solution)/shard_map/ppermute | solution.py:21
  50.7 9.2 %collective-permute-start.6 = (s32[128]{0:T(128)S(1)}, s32[128]{0:T(128)S(1)}, u32[]{:S(2)}, u32[]{:S(2)}) collective-permute-start(s32[128]{0:T(128)S(1)} %collective-permute-done.5), channel_id=1, source_target_pairs={{0,1},{1,2},{2,3},{3,4},{4,5},{5,6},{6,7},{7,0},{8,9},{9,10},{10,1... | collective-permute-start | bytes 1544 | tf_op jit(solution)/shard_map/ppermute | solution.py:21
  55.4 11.5 %collective-permute-start.8 = (bf16[128,1600]{0,1:T(8,128)(2,1)}, bf16[128,1600]{0,1:T(8,128)(2,1)}, u32[]{:S(2)}, u32[]{:S(2)}) collective-permute-start(bf16[128,1600]{0,1:T(8,128)(2,1)} %collective-permute-done.7), channel_id=1, source_target_pairs={{0,7},{1,0},{2,1},{3,2},{4,3},{5,4},{6,5},{7,6},{8,15},{9,8},{10,9... | collective-permute-start | bytes 1228808 | tf_op jit(solution)/shard_map/ppermute | solution.py:21
  59.9 42.1 %collective-permute-start.12 = (bf16[128,1600]{0,1:T(8,128)(2,1)}, bf16[128,1600]{0,1:T(8,128)(2,1)}, u32[]{:S(2)}, u32[]{:S(2)}) collective-permute-start(bf16[128,1600]{0,1:T(8,128)(2,1)} %collective-permute-done.11), channel_id=1, source_target_pairs={{0,1},{1,2},{2,3},{3,4},{4,5},{5,6},{6,7},{7,0},{8,9},{9,10},{10,1... | collective-permute-start | bytes 1228808 | tf_op jit(solution)/shard_map/ppermute | solution.py:21
  66.9 38.8 %collective-permute-start.9 = (bf16[128,1600]{0,1:T(8,128)(2,1)}, bf16[128,1600]{0,1:T(8,128)(2,1)}, u32[]{:S(2)}, u32[]{:S(2)}) collective-permute-start(bf16[128,1600]{0,1:T(8,128)(2,1)} %collective-permute-done.8), channel_id=1, source_target_pairs={{0,7},{1,0},{2,1},{3,2},{4,3},{5,4},{6,5},{7,6},{8,15},{9,8},{10,9... | collective-permute-start | bytes 1228808 | tf_op jit(solution)/shard_map/ppermute | solution.py:21
  98.2 30.2 %collective-permute-start.14 = (bf16[1024,1600]{0,1:T(8,128)(2,1)}, bf16[1024,1600]{0,1:T(8,128)(2,1)S(1)}, u32[]{:S(2)}, u32[]{:S(2)}) collective-permute-start(bf16[1024,1600]{0,1:T(8,128)(2,1)} %copy.9), channel_id=1, source_target_pairs={{0,8},{8,0},{1,9},{9,1},{2,10},{10,2},{3,11},{11,3},{4,12},{12,4},... | collective-permute-start | bytes 9830408 | tf_op jit(solution)/shard_map/ppermute | solution.py:21
  102.0 14.0 %collective-permute-start.13 = (bf16[128,1600]{0,1:T(8,128)(2,1)}, bf16[128,1600]{0,1:T(8,128)(2,1)S(1)}, u32[]{:S(2)}, u32[]{:S(2)}) collective-permute-start(bf16[128,1600]{0,1:T(8,128)(2,1)} %collective-permute-done.12), channel_id=1, source_target_pairs={{0,1},{1,2},{2,3},{3,4},{4,5},{5,6},{6,7},{7,0},{8,9},{9,10},{10,1... | collective-permute-start | bytes 1228808 | tf_op jit(solution)/shard_map/ppermute | solution.py:21
  122.2 1.9 %copy-start = (bf16[1024,1600]{0,1:T(8,128)(2,1)S(1)}, bf16[1024,1600]{0,1:T(8,128)(2,1)}, u32[]{:S(2)}) copy-start(bf16[1024,1600]{0,1:T(8,128)(2,1)} %constant_dynamic-update-slice_fusion.1) | copy-start | bytes 9830404
  132.7 38.1 %copy-start.2 = (s32[128]{0:T(128)S(1)}, s32[128]{0:T(128)}, u32[]{:S(2)}) copy-start(s32[128]{0:T(128)} %param.9) | copy-start | bytes 1540
  136.6 20.5 %collective-permute-start.15 = (f32[4,128]{1,0:T(4,128)S(1)}, f32[4,128]{1,0:T(4,128)S(1)}, u32[]{:S(2)}, u32[]{:S(2)}) collective-permute-start(f32[4,128]{1,0:T(4,128)S(1)} %bitcast.602), channel_id=1, source_target_pairs={{0,1},{1,2},{2,3},{3,4},{4,5},{5,6},{6,7},{7,0},{8,9},{9,10},{10,1... | collective-permute-start | bytes 6152 | tf_op jit(solution)/shard_map/ppermute | solution.py:21
  140.1 24.1 %collective-permute-start.18 = (f32[4,128]{1,0:T(4,128)S(1)}, f32[4,128]{1,0:T(4,128)S(1)}, u32[]{:S(2)}, u32[]{:S(2)}) collective-permute-start(f32[4,128]{1,0:T(4,128)S(1)} %bitcast.601), channel_id=1, source_target_pairs={{0,4},{1,5},{2,6},{3,7},{4,0},{5,1},{6,2},{7,3},{8,12},{9,13},{10,... | collective-permute-start | bytes 6152 | tf_op jit(solution)/shard_map/ppermute | solution.py:21
  147.3 18.8 %collective-permute-start.19 = (f32[4,128]{1,0:T(4,128)S(1)}, f32[4,128]{1,0:T(4,128)S(1)}, u32[]{:S(2)}, u32[]{:S(2)}) collective-permute-start(f32[4,128]{1,0:T(4,128)S(1)} %bitcast.600), channel_id=1, source_target_pairs={{0,5},{1,6},{2,7},{3,0},{4,1},{5,2},{6,3},{7,4},{8,13},{9,14},{10,... | collective-permute-start | bytes 6152 | tf_op jit(solution)/shard_map/ppermute | solution.py:21
  149.2 16.9 %collective-permute-start.20 = (f32[4,128]{1,0:T(4,128)S(1)}, f32[4,128]{1,0:T(4,128)S(1)}, u32[]{:S(2)}, u32[]{:S(2)}) collective-permute-start(f32[4,128]{1,0:T(4,128)S(1)} %bitcast.599), channel_id=1, source_target_pairs={{0,6},{1,7},{2,0},{3,1},{4,2},{5,3},{6,4},{7,5},{8,14},{9,15},{10,... | collective-permute-start | bytes 6152 | tf_op jit(solution)/shard_map/ppermute | solution.py:21
  152.3 13.8 %collective-permute-start.16 = (f32[4,128]{1,0:T(4,128)S(1)}, f32[4,128]{1,0:T(4,128)S(1)}, u32[]{:S(2)}, u32[]{:S(2)}) collective-permute-start(f32[4,128]{1,0:T(4,128)S(1)} %bitcast.605), channel_id=1, source_target_pairs={{0,2},{1,3},{2,4},{3,5},{4,6},{5,7},{6,0},{7,1},{8,10},{9,11},{10,... | collective-permute-start | bytes 6152 | tf_op jit(solution)/shard_map/ppermute | solution.py:21
  157.2 8.9 %collective-permute-start.17 = (f32[4,128]{1,0:T(4,128)S(1)}, f32[4,128]{1,0:T(4,128)S(1)}, u32[]{:S(2)}, u32[]{:S(2)}) collective-permute-start(f32[4,128]{1,0:T(4,128)S(1)} %bitcast.604), channel_id=1, source_target_pairs={{0,3},{1,4},{2,5},{3,6},{4,7},{5,0},{6,1},{7,2},{8,11},{9,12},{10,... | collective-permute-start | bytes 6152 | tf_op jit(solution)/shard_map/ppermute | solution.py:21
  164.1 6.7 %collective-permute-start.21 = (f32[4,128]{1,0:T(4,128)S(1)}, f32[4,128]{1,0:T(4,128)S(1)}, u32[]{:S(2)}, u32[]{:S(2)}) collective-permute-start(f32[4,128]{1,0:T(4,128)S(1)} %bitcast.603), channel_id=1, source_target_pairs={{0,7},{1,0},{2,1},{3,2},{4,3},{5,4},{6,5},{7,6},{8,15},{9,8},{10,9... | collective-permute-start | bytes 6152 | tf_op jit(solution)/shard_map/ppermute | solution.py:21
